TPU v7x, 128 devices: a whole 4x4x4 slice. The times are simulated.
128 devices in a mesh: req: 16 (over y, z), mlp: 8 (over x, core).
Axes of the slice: x: 4, y: 4, z: 4, core: 2. Of those that a mesh axis runs over, the one named last changes fastest.
Arguments:
- resid: bfloat16 [2176, 5120], P('req', 'mlp'), may hold values from -180 to 180
- queries: bfloat16 [2176, 5120], P('req', 'mlp'), may hold values from -200 to 200
- new_keys: bfloat16 [2176, 1024], P('req', 'mlp'), may hold values from -6 to 6
- new_values: bfloat16 [2176, 1024], P('req', 'mlp'), may hold values from -6 to 6
- cache_keys: bfloat16 [48, 4096, 1024], P('req', None, 'mlp'), may hold values from -6 to 6
- cache_values: bfloat16 [48, 4096, 1024], P('req', None, 'mlp'), may hold values from -6 to 6
- context_keys: bfloat16 [5, 1024, 1024], P(None, 'req', 'mlp'), may hold values from -6 to 6
- context_values: bfloat16 [5, 1024, 1024], P(None, 'req', 'mlp'), may hold values from -6 to 6
- cache_lengths: int32 [48], P('req'), may hold values from 1 to 4096, 49152 in all
- group_ids: int32 [48], P('req'), may hold values from 0 to 3
- prefix_lengths: int32 [4], replicated, may hold values from 1 to 1024, 2048 in all
- prompt_start: int32 [1], replicated, may hold values from 1 to 1023
- out_weight: bfloat16 [5120, 5120], P('mlp'), may hold values from -1.25 to 1.25
- norm_gain: float32 [5120], P('mlp'), may hold values from 0.5 to 1.5
- gate_weight: bfloat16 [5120, 27648], P(None, ('req', 'mlp')), may hold values from -0.078125 to 0.078125
- up_weight: bfloat16 [5120, 27648], P(None, ('req', 'mlp')), may hold values from -0.078125 to 0.078125
- down_weight: bfloat16 [27648, 5120], P('req', 'mlp'), may hold values from -0.109375 to 0.109375
Outputs:
- out: bfloat16 [2176, 5120], P('req', 'mlp')
Inputs may be any that keep to these rules, and one draw needn't show every extreme that they name: `cache_lengths`: one decode request has 4096 valid positions. `prefix_lengths`: one group's prompt has 1024 positions.
All inputs are finite; a program needn't handle non-finite values. No bound on the sum of `cache_lengths` on one device may be relied on, other than what follows from the above.
Results may differ from a plain program's by a relative error of at most 0.019.
Values may be sent and summed in bfloat16 or wider, within the bound.
No kernel may reach another device: no remote copies, remote signals or barrier semaphores. Data moves between devices by JAX's collectives and lax.ppermute only.
A program may use at most 128 MiB of HBM per device.

v0:
```python
import math
import jax
import jax.numpy as jnp
from jax import lax
from jax.sharding import PartitionSpec as P

D = 5120
HQ = 40
KV = 8
HD = 128
NEGATIVE = -1e30


def absorb(carried, scores, allowed, values, pattern):
    running, totals, summed = carried
    scores = jnp.where(allowed, scores, -jnp.inf)
    highest = jnp.maximum(running, jnp.max(scores, axis=-1))
    exponent = jnp.where(allowed, jnp.exp(scores - highest[..., None]), 0.0)
    fading = jnp.exp(running - highest)
    weights = exponent.astype(jnp.bfloat16)
    summed = summed * fading[..., None] + jnp.einsum(
        pattern, weights, values, preferred_element_type=jnp.float32
    )
    totals = totals * fading + jnp.sum(exponent, axis=-1)
    return (highest, totals, summed)


def per_device(
    resid,
    queries,
    new_keys,
    new_values,
    cache_keys,
    cache_values,
    context_keys,
    context_values,
    cache_lengths,
    group_ids,
    prefix_lengths,
    prompt_start,
    out_weight,
    norm_gain,
    gate_weight,
    up_weight,
    down_weight,
):
    rows_here = queries.shape[0]
    decode_count = cache_keys.shape[0]
    prompt_count = rows_here - decode_count
    heads_kv = new_keys.shape[1] // HD
    group_size = HQ // KV
    scaling = 1.0 / math.sqrt(HD)
    cache_span = cache_keys.shape[1]
    context_count = context_keys.shape[0]
    query_rows = queries.reshape(rows_here, heads_kv, group_size, HD)
    query_decode = query_rows[:decode_count]
    query_prompt = query_rows[decode_count:]
    key_rows = new_keys.reshape(rows_here, heads_kv, HD)
    value_rows = new_values.reshape(rows_here, heads_kv, HD)

    def fresh_state(row_count):
        return (
            jnp.full((row_count, heads_kv, group_size), NEGATIVE, jnp.float32),
            jnp.zeros((row_count, heads_kv, group_size), jnp.float32),
            jnp.zeros((row_count, heads_kv, group_size, HD), jnp.float32),
        )

    past_keys = cache_keys.reshape(decode_count, cache_span, heads_kv, HD)
    past_values = cache_values.reshape(decode_count, cache_span, heads_kv, HD)
    scores = (
        jnp.einsum("ikgd,ickd->ikgc", query_decode, past_keys, preferred_element_type=jnp.float32)
        * scaling
    )
    usable = (jnp.arange(cache_span)[None, :] < cache_lengths[:, None])[:, None, None, :]
    decode_state = absorb(fresh_state(decode_count), scores, usable, past_values, "ikgc,ickd->ikgd")
    own_scores = (
        jnp.einsum(
            "ikgd,ikd->ikg",
            query_decode,
            key_rows[:decode_count],
            preferred_element_type=jnp.float32,
        )[..., None]
        * scaling
    )
    decode_state = absorb(
        decode_state,
        own_scores,
        jnp.ones(own_scores.shape, dtype=bool),
        value_rows[:decode_count][:, None],
        "ikgc,ickd->ikgd",
    )
    prompt_length = prompt_start[0]
    prefix_here = prefix_lengths[group_ids]
    state_decode = decode_state
    state_prompt = fresh_state(prompt_count)
    req_count = lax.axis_size("req")
    context_rows = context_keys.shape[1]
    packed = jnp.concatenate(
        [
            context_keys.reshape(context_count * context_rows, heads_kv * HD),
            context_values.reshape(context_count * context_rows, heads_kv * HD),
            new_keys,
            new_values,
        ],
        0,
    )
    gathered = lax.all_gather(packed, "req", axis=0, tiled=False)
    context_span = context_count * context_rows

    def context_of(offset):
        piece = gathered[:, offset : offset + context_span]
        piece = piece.reshape(req_count, context_count, context_rows, heads_kv * HD)
        return jnp.transpose(piece, (1, 0, 2, 3)).reshape(
            context_count, req_count * context_rows, heads_kv * HD
        )

    def prompt_of(offset):
        piece = gathered[:, offset : offset + rows_here][:, decode_count:]
        return piece.reshape(req_count * prompt_count, heads_kv * HD)

    key_block = context_of(0)
    value_block = context_of(context_span)
    extent = key_block.shape[1]
    positions = jnp.arange(extent)
    key_split = key_block.reshape(context_count, extent, heads_kv, HD)
    value_split = value_block.reshape(context_count, extent, heads_kv, HD)
    chosen_keys = key_split[group_ids]
    chosen_values = value_split[group_ids]
    block_scores = (
        jnp.einsum("ikgd,ickd->ikgc", query_decode, chosen_keys, preferred_element_type=jnp.float32)
        * scaling
    )
    block_usable = (positions[None, :] < prefix_here[:, None])[:, None, None, :]
    state_decode = absorb(
        state_decode, block_scores, block_usable, chosen_values, "ikgc,ickd->ikgd"
    )
    block_scores = (
        jnp.einsum(
            "jkgd,ckd->jkgc",
            query_prompt,
            key_split[context_count - 1],
            preferred_element_type=jnp.float32,
        )
        * scaling
    )
    block_usable = (positions < prompt_length)[None, None, None, :]
    state_prompt = absorb(
        state_prompt, block_scores, block_usable, value_split[context_count - 1], "jkgc,ckd->jkgd"
    )
    prompt_state = state_prompt
    own_positions = lax.axis_index("req") * prompt_count + jnp.arange(prompt_count, dtype=jnp.int32)
    key_block = prompt_of(2 * context_span)
    value_block = prompt_of(2 * context_span + rows_here)
    extent = key_block.shape[0]
    positions = jnp.arange(extent, dtype=jnp.int32)
    block_scores = (
        jnp.einsum(
            "jkgd,ckd->jkgc",
            query_prompt,
            key_block.reshape(extent, heads_kv, HD),
            preferred_element_type=jnp.float32,
        )
        * scaling
    )
    block_usable = (positions[None, :] <= own_positions[:, None])[:, None, None, :]
    prompt_state = absorb(
        prompt_state,
        block_scores,
        block_usable,
        value_block.reshape(extent, heads_kv, HD),
        "jkgc,ckd->jkgd",
    )

    def finish(carried):
        return (carried[2] / carried[1][..., None]).astype(jnp.bfloat16)

    attended = jnp.concatenate([finish(state_decode), finish(prompt_state)], 0).reshape(
        rows_here, heads_kv * group_size * HD
    )
    mlp_count = lax.axis_size("mlp")
    head_partial = jnp.dot(attended, out_weight, preferred_element_type=jnp.float32)
    pieces = lax.all_to_all(head_partial.astype(jnp.bfloat16), "mlp", 1, 0, tiled=True)
    projected = jnp.sum(pieces.reshape(mlp_count, rows_here, -1).astype(jnp.float32), axis=0)
    mixed = (resid.astype(jnp.float32) + projected).astype(jnp.bfloat16)
    mixed_wide = mixed.astype(jnp.float32)
    gain_pieces = []
    remainder = norm_gain
    for _ in range(3):
        piece = remainder.astype(jnp.bfloat16)
        gain_pieces.append(piece)
        remainder = remainder - piece.astype(jnp.float32)
    with_gain = jnp.concatenate([mixed, jnp.stack(gain_pieces, 0)], 0)
    gathered_rows = lax.all_gather(with_gain, "mlp", axis=1, tiled=True).astype(jnp.float32)
    mixed_rows = gathered_rows[:rows_here]
    full_gain = (
        gathered_rows[rows_here] + gathered_rows[rows_here + 1] + gathered_rows[rows_here + 2]
    )
    square_total = jnp.sum(mixed_rows * mixed_rows, axis=1)
    half = D // 2
    side = lax.axis_index("mlp") % 2
    own_half = lax.dynamic_slice_in_dim(mixed_rows, side * half, half, axis=1)
    own_gain = lax.dynamic_slice_in_dim(full_gain, side * half, half, axis=0)
    normed = (own_half * lax.rsqrt(square_total / D + 1e-06)[:, None] * own_gain[None, :]).astype(
        jnp.bfloat16
    )
    pairs = [(i, i ^ 1) for i in range(mlp_count)]

    def halves(weight):
        return (
            lax.dynamic_slice_in_dim(weight, side * half, half, axis=0),
            lax.dynamic_slice_in_dim(weight, (1 - side) * half, half, axis=0),
        )

    gate_near, gate_far = halves(gate_weight)
    up_near, up_far = halves(up_weight)
    chunk_count = 2
    chunk_rows = rows_here // chunk_count
    feeds = []
    for chunk in range(chunk_count):
        rows = normed[chunk * chunk_rows : (chunk + 1) * chunk_rows]
        near_rows = lax.all_gather(rows, "req", axis=0, tiled=True)
        far_rows = lax.ppermute(near_rows, "mlp", pairs)
        gate_proj = jnp.dot(near_rows, gate_near, preferred_element_type=jnp.float32) + jnp.dot(
            far_rows, gate_far, preferred_element_type=jnp.float32
        )
        up_proj = jnp.dot(near_rows, up_near, preferred_element_type=jnp.float32) + jnp.dot(
            far_rows, up_far, preferred_element_type=jnp.float32
        )
        hidden = (jax.nn.silu(gate_proj) * up_proj).astype(jnp.bfloat16)
        hidden_block = lax.all_gather(hidden, "mlp", axis=1, tiled=True)
        down_partial = jnp.dot(hidden_block, down_weight, preferred_element_type=jnp.float32)
        req_pieces = lax.all_to_all(down_partial.astype(jnp.bfloat16), "req", 0, 0, tiled=True)
        feeds.append(
            jnp.sum(req_pieces.reshape(req_count, chunk_rows, -1).astype(jnp.float32), axis=0)
        )
    feed = jnp.concatenate(feeds, 0)
    return (mixed_wide + feed).astype(jnp.bfloat16)


def solution(mesh):
    return jax.shard_map(
        per_device,
        mesh=mesh,
        in_specs=(
            P("req", "mlp"),
            P("req", "mlp"),
            P("req", "mlp"),
            P("req", "mlp"),
            P("req", None, "mlp"),
            P("req", None, "mlp"),
            P(None, "req", "mlp"),
            P(None, "req", "mlp"),
            P("req"),
            P("req"),
            P(),
            P(),
            P("mlp", None),
            P("mlp"),
            P(None, ("req", "mlp")),
            P(None, ("req", "mlp")),
            P("req", "mlp"),
        ),
        out_specs=P("req", "mlp"),
        check_vma=False,
    )
```

profile of v0, /device:TPU:0, one launch (start us, length us, event | category | flops | bytes accessed | tf_op | source)
XLA Modules:
  0.0 399.9 jit_solution(140865241295268066)
XLA Ops:
  6.5 1.8 pad_maximum_fusion
  9.1 1.0 slice.64
  12.9 1.3 gather_fusion
  15.5 1.3 slice_convert_fusion
  18.9 2.3 fusion.114
  21.4 40.6 %all-gather.16.cloned.1.call-done = bf16[14592,128]{1,0:T(8,128)(2,1)} async-done(((bf16[912,128]{1,0:T(8,128)(2,1)}), bf16[14592,128]{1,0:T(8,128)(2,1)}) %all-gather.16.cloned.1.call-update) | async-done | bytes 3735568 | tf_op jit(solution)/shard_map/all_gather | solution.py:107
  62.0 1.9 fusion.110
  63.9 2.6 fusion.109
  66.5 1.2 copy.26
  68.4 1.2 copy.27
  70.4 1.7 gather_fusion.1
  72.0 2.1 gather_fusion.2
  74.2 1.6 fusion.115
  76.6 2.5 fusion.45
  79.3 1.0 reshape.441
  80.3 1.3 fusion.113
  82.3 1.4 fusion
  85.8 1.4 fusion.52
  88.1 1.3 convolution_convert_fusion
  89.4 1.2 copy.75
  90.6 4.4 %all-to-all-start = ((bf16[136,8,640]{2,0,1:T(8,128)(2,1)}), bf16[136,8,640]{2,0,1:T(8,128)(2,1)S(1)}, u32[]{:S(2)}, u32[]{:S(2)}) async-start(bf16[136,8,640]{2,0,1:T(8,128)(2,1)} %bitcast.172), calls=%async_computation | async-start | bytes 2785280 | tf_op jit(solution)/shard_map/all_to_all | solution.py:182
  95.3 19.3 %all-to-all-done = bf16[136,8,640]{2,0,1:T(8,128)(2,1)S(1)} async-done(((bf16[136,8,640]{2,0,1:T(8,128)(2,1)}), bf16[136,8,640]{2,0,1:T(8,128)(2,1)S(1)}, u32[]{:S(2)}, u32[]{:S(2)}) %all-to-all-start) | async-done | bytes 1392672 | tf_op jit(solution)/shard_map/all_to_all | solution.py:182
  115.6 21.5 %all-gather.10.cloned.1.call-done = bf16[139,5120]{1,0:T(8,128)(2,1)} async-done(((bf16[139,640]{1,0:T(8,128)(2,1)}), bf16[139,5120]{1,0:T(8,128)(2,1)}) %all-gather.10.cloned.1.call-update) | async-done | bytes 1423376 | tf_op jit(solution)/shard_map/all_gather | solution.py:193
  137.2 1.8 convert_element_type.97
  139.8 0.9 slice_bitcast_fusion.1
  141.4 59.1 %all-gather.18.cloned.1.call-done = bf16[16,68,2560]{2,1,0:T(8,128)(2,1)} async-done(((bf16[1,68,2560]{2,1,0:T(8,128)(2,1)}), bf16[16,68,2560]{2,1,0:T(8,128)(2,1)}) %all-gather.18.cloned.1.call-update) | async-done | bytes 5570576 | tf_op jit(solution)/shard_map/all_gather | solution.py:221
  200.5 7.9 %reshape.433 = bf16[1088,2560]{1,0:T(8,128)(2,1)} reshape(bf16[16,68,2560]{2,1,0:T(8,128)(2,1)} %all-gather.18.cloned.1.call-done) | data formatting | bytes 11141120
  208.4 53.3 %all-gather.20.cloned.1.call-done = bf16[16,68,2560]{2,1,0:T(8,128)(2,1)} async-done(((bf16[1,68,2560]{2,1,0:T(8,128)(2,1)}), bf16[16,68,2560]{2,1,0:T(8,128)(2,1)}) %all-gather.20.cloned.1.call-update) | async-done | bytes 5570576 | tf_op jit(solution)/shard_map/all_gather | solution.py:221
  261.7 7.9 %reshape.435 = bf16[1088,2560]{1,0:T(8,128)(2,1)} reshape(bf16[16,68,2560]{2,1,0:T(8,128)(2,1)} %all-gather.20.cloned.1.call-done) | data formatting | bytes 11141120
  269.6 4.7 %fusion.65 = f32[1088,216]{0,1:T(8,128)S(1)} fusion(bf16[1088,2560]{1,0:T(8,128)(2,1)} %reshape.433, bf16[5120,216]{0,1:T(8,128)(2,1)S(1)} %copy-done.21, s32[]{:T(128)S(6)} %select_n.78), kind=kOutput, calls=%fused_computation.72 | convolution fusion | flops 1203240960 | bytes 7616516 | tf_op jit(solution)/shard_map/dot_general | solution.py:223
  274.5 2.0 fusion.59
  276.5 4.6 %convolution_add_fusion.3 = f32[1088,216]{0,1:T(8,128)S(1)} fusion(f32[1088,216]{0,1:T(8,128)S(1)} %fusion.65, bf16[1088,2560]{1,0:T(8,128)(2,1)} %collective-permute-done, bf16[5120,216]{0,1:T(8,128)(2,1)S(1)} %copy-done.21, s32[]{:T(128)S(6)} %select_n.79), kind=kOutput, calls=%fused_computation.31 | convolution fusion | flops 1203475968 | bytes 8611844 | tf_op jit(solution)/shard_map/dot_general | solution.py:223
  281.1 5.5 %fusion.13 = bf16[1088,216]{0,1:T(8,128)(2,1)} fusion(f32[1088,216]{0,1:T(8,128)S(1)} %fusion.59, bf16[1088,2560]{1,0:T(8,128)(2,1)} %collective-permute-done, f32[1088,216]{0,1:T(8,128)S(1)} %convolution_add_fusion.3, bf16[5120,216]{0,1:T(8,128)(2,1)S(1)} %copy-done.22, s32[]{:T(128)S(6)} %select_n.79), kind=kOutput, calls=%fused_computation.32 | convolution fusion | flops 1204886016 | bytes 9137156 | tf_op jit(solution)/shard_map/dot_general | solution.py:226
  286.9 4.7 %fusion.63 = f32[1088,216]{0,1:T(8,128)S(1)} fusion(bf16[1088,2560]{1,0:T(8,128)(2,1)} %reshape.435, bf16[5120,216]{0,1:T(8,128)(2,1)S(1)} %copy-done.21, s32[]{:T(128)S(6)} %select_n.78), kind=kOutput, calls=%fused_computation.70 | convolution fusion | flops 1203240960 | bytes 7616516 | tf_op jit(solution)/shard_map/dot_general | solution.py:223
  291.6 4.6 %fusion.57 = f32[1088,216]{0,1:T(8,128)S(1)} fusion(bf16[1088,2560]{1,0:T(8,128)(2,1)} %reshape.435, bf16[5120,216]{0,1:T(8,128)(2,1)S(1)} %copy-done.23, s32[]{:T(128)S(6)} %select_n.78), kind=kOutput, calls=%fused_computation.64 | convolution fusion | flops 1203240960 | bytes 7616516 | tf_op jit(solution)/shard_map/dot_general | solution.py:226
  296.2 4.9 %convolution_add_fusion.1 = f32[1088,216]{0,1:T(8,128)S(1)} fusion(f32[1088,216]{0,1:T(8,128)S(1)} %fusion.63, bf16[1088,2560]{1,0:T(8,128)(2,1)} %collective-permute-done.1, bf16[5120,216]{0,1:T(8,128)(2,1)S(1)} %copy-done.21, s32[]{:T(128)S(6)} %select_n.79), kind=kOutput, calls=%fused_computation.28 | convolution fusion | flops 1203475968 | bytes 8611844 | tf_op jit(solution)/shard_map/dot_general | solution.py:223
  301.2 5.5 %fusion.14 = bf16[1088,216]{0,1:T(8,128)(2,1)} fusion(f32[1088,216]{0,1:T(8,128)S(1)} %fusion.57, bf16[1088,2560]{1,0:T(8,128)(2,1)} %collective-permute-done.1, f32[1088,216]{0,1:T(8,128)S(1)} %convolution_add_fusion.1, bf16[5120,216]{0,1:T(8,128)(2,1)S(1)} %copy-done.23, s32[]{:T(128)S(6)} %select_n.79), kind=kOutput, calls=%fused_computation.33 | convolution fusion | flops 1204886016 | bytes 9137156 | tf_op jit(solution)/shard_map/dot_general | solution.py:226
  306.7 10.9 %all-gather.12.cloned.1.call-done = bf16[1088,1728]{0,1:T(8,128)(2,1)} async-done(((bf16[1088,216]{0,1:T(8,128)(2,1)}), bf16[1088,1728]{0,1:T(8,128)(2,1)}) %all-gather.12.cloned.1.call-update) | async-done | bytes 3760144 | tf_op jit(solution)/shard_map/all_gather | solution.py:230
  317.6 6.1 %convolution_convert_fusion.2 = bf16[1088,640]{1,0:T(8,128)(2,1)S(1)} fusion(bf16[1088,1728]{0,1:T(8,128)(2,1)} %all-gather.12.cloned.1.call-done, bf16[1728,640]{1,0:T(8,128)(2,1)} %param.33), kind=kOutput, calls=%fused_computation.11 | convolution fusion | flops 2407178240 | bytes 7364608 | tf_op jit(solution)/shard_map/dot_general | solution.py:231
  323.7 1.3 all_to_all.24
  325.0 7.2 %all-to-all-start.1 = ((bf16[16,68,640]{2,1,0:T(8,128)(2,1)}), bf16[16,68,640]{2,1,0:T(8,128)(2,1)}, u32[]{:S(2)}, u32[]{:S(2)}) async-start(bf16[16,68,640]{2,1,0:T(8,128)(2,1)} %all_to_all.24), calls=%async_computation.1 | async-start | bytes 2949120 | tf_op jit(solution)/shard_map/all_to_all | solution.py:232
  332.2 18.1 %all-gather.14.cloned.1.call-done = bf16[1088,1728]{0,1:T(8,128)(2,1)} async-done(((bf16[1088,216]{0,1:T(8,128)(2,1)}), bf16[1088,1728]{0,1:T(8,128)(2,1)}) %all-gather.14.cloned.1.call-update) | async-done | bytes 3760144 | tf_op jit(solution)/shard_map/all_gather | solution.py:230
  350.3 6.6 %convolution_convert_fusion.1 = bf16[1088,640]{1,0:T(8,128)(2,1)} fusion(bf16[1088,1728]{0,1:T(8,128)(2,1)} %all-gather.14.cloned.1.call-done, bf16[1728,640]{1,0:T(8,128)(2,1)S(1)} %copy-done.24), kind=kOutput, calls=%fused_computation.10 | convolution fusion | flops 2407178240 | bytes 7364608 | tf_op jit(solution)/shard_map/dot_general | solution.py:231
  356.9 3.4 all_to_all.26
  360.3 7.0 %all-to-all-start.2 = ((bf16[16,68,640]{2,1,0:T(8,128)(2,1)}), bf16[16,68,640]{2,1,0:T(8,128)(2,1)}, u32[]{:S(2)}, u32[]{:S(2)}) async-start(bf16[16,68,640]{2,1,0:T(8,128)(2,1)} %all_to_all.26), calls=%async_computation.2 | async-start | bytes 2949120 | tf_op jit(solution)/shard_map/all_to_all | solution.py:232
  367.3 1.6 convert_reduce_fusion.1
  368.9 21.8 %all-to-all-done.2 = bf16[16,68,640]{2,1,0:T(8,128)(2,1)} async-done(((bf16[16,68,640]{2,1,0:T(8,128)(2,1)}), bf16[16,68,640]{2,1,0:T(8,128)(2,1)}, u32[]{:S(2)}, u32[]{:S(2)}) %all-to-all-start.2) | async-done | bytes 1392672 | tf_op jit(solution)/shard_map/all_to_all | solution.py:232
  390.7 1.6 convert_reduce_fusion
  (115 shorter events, 16.3 us)
Async XLA Ops:
  6.5 12.3 %copy-start = (bf16[3,4096,128]{2,1,0:T(8,128)(2,1)S(1)}, bf16[3,4096,128]{2,1,0:T(8,128)(2,1)}, u32[]{:S(2)}) copy-start(bf16[3,4096,128]{2,1,0:T(8,128)(2,1)} %param.21) | copy-start | bytes 9437188
  6.5 55.5 %all-gather.16.cloned.1.call-start = ((), (), s32[]{:S(2)}) async-start(), calls=%async_computation.6 | async-start | bytes 3969024 | tf_op jit(solution)/shard_map/all_gather | solution.py:107
  10.1 8.0 %copy-start.14 = (bf16[3,5,128]{2,1,0:T(8,128)(2,1)}, bf16[3,5,128]{2,1,0:T(8,128)(2,1)S(1)}, u32[]{:S(2)}) copy-start(bf16[3,5,128]{2,1,0:T(8,128)(2,1)S(1)} %reshape.382) | copy-start | bytes 11524
  68.4 1.9 copy-start.4
  68.4 5.7 %copy-start.13 = (pred[3,1024]{1,0:T(4,128)(4,1)S(1)}, pred[3,1024]{1,0:T(4,128)(4,1)}, u32[]{:S(2)}) copy-start(pred[3,1024]{1,0:T(4,128)(4,1)} %iota_compare_fusion.2) | copy-start | bytes 9220
  68.4 5.8 %copy-start.15 = (bf16[3,5,128]{2,1,0:T(8,128)(2,1)S(1)}, bf16[3,5,128]{2,1,0:T(8,128)(2,1)}, u32[]{:S(2)}) copy-start(bf16[3,5,128]{2,1,0:T(8,128)(2,1)} %copy-done.14) | copy-start | bytes 11524
  69.6 6.2 %copy-start.16 = (f32[3,5]{1,0:T(4,128)S(1)}, f32[3,5]{1,0:T(4,128)}, u32[]{:S(2)}) copy-start(f32[3,5]{1,0:T(4,128)} %get-tuple-element.34) | copy-start | bytes 184
  69.6 6.2 %copy-start.19 = (f32[3,1,5]{2,1,0:T(1,128)S(1)}, f32[3,1,5]{2,1,0:T(1,128)}, u32[]{:S(2)}) copy-start(f32[3,1,5]{2,1,0:T(1,128)} %fusion.98) | copy-start | bytes 184
  70.4 6.2 %copy-start.18 = (f32[3,128]{1,0:T(4,128)S(1)}, f32[3,128]{1,0:T(4,128)}, u32[]{:S(2)}) copy-start(f32[3,128]{1,0:T(4,128)} %slice_convert_fusion) | copy-start | bytes 4612
  74.2 4.9 %copy-start.6 = (bf16[16,133,128]{2,1,0:T(8,128)(2,1)S(1)}, bf16[16,133,128]{2,1,0:T(8,128)(2,1)}, u32[]{:S(2)}) copy-start(bf16[16,133,128]{2,1,0:T(8,128)(2,1)} %get-tuple-element.8) | copy-start | bytes 1634308
  76.3 3.0 copy-start.5
  76.6 3.7 copy-start.7
  80.3 1.3 copy-start.8
  80.3 1.4 copy-start.9
  80.3 1.4 copy-start.17
  83.8 1.0 copy-start.11
  84.8 1.0 copy-start.10
  84.8 2.6 slice-start
  85.8 2.3 slice-start.1
  89.3 5.9 %copy-start.20 = (f32[640]{0:T(1024)S(1)}, f32[640]{0:T(1024)}, u32[]{:S(2)}) copy-start(f32[640]{0:T(1024)} %param.30) | copy-start | bytes 7684
  90.6 24.2 %copy-start.12 = (bf16[136,640]{1,0:T(8,128)(2,1)S(1)}, bf16[136,640]{1,0:T(8,128)(2,1)}, u32[]{:S(2)}) copy-start(bf16[136,640]{1,0:T(8,128)(2,1)} %param.17) | copy-start | bytes 522244
  90.6 24.0 %all-to-all-start = ((bf16[136,8,640]{2,0,1:T(8,128)(2,1)}), bf16[136,8,640]{2,0,1:T(8,128)(2,1)S(1)}, u32[]{:S(2)}, u32[]{:S(2)}) async-start(bf16[136,8,640]{2,0,1:T(8,128)(2,1)} %bitcast.172), calls=%async_computation | async-start | bytes 2785280 | tf_op jit(solution)/shard_map/all_to_all | solution.py:182
  95.0 42.2 %all-gather.10.cloned.1.call-start = ((), (), s32[]{:S(2)}) async-start(), calls=%async_computation.3 | async-start | bytes 1658880 | tf_op jit(solution)/shard_map/all_gather | solution.py:193
  115.6 84.9 %all-gather.18.cloned.1.call-start = ((), (), s32[]{:S(2)}) async-start(), calls=%async_computation.7 | async-start | bytes 6266880 | tf_op jit(solution)/shard_map/all_gather | solution.py:221
  137.1 2.1 copy-start.2
  140.8 120.9 %all-gather.20.cloned.1.call-start = ((), (), s32[]{:S(2)}) async-start(), calls=%async_computation.8 | async-start | bytes 6266880 | tf_op jit(solution)/shard_map/all_gather | solution.py:221
  141.3 176.3 %all-gather.12.cloned.1.call-start = ((), (), s32[]{:S(2)}) async-start(), calls=%async_computation.4 | async-start | bytes 4478976 | tf_op jit(solution)/shard_map/all_gather | solution.py:230
  208.4 68.1 %collective-permute-start = (bf16[1088,2560]{1,0:T(8,128)(2,1)}, bf16[1088,2560]{1,0:T(8,128)(2,1)}, u32[]{:S(2)}, u32[]{:S(2)}) collective-permute-start(bf16[1088,2560]{1,0:T(8,128)(2,1)} %reshape.433), channel_id=1, source_target_pairs={{0,1},{1,0},{2,3},{3,2},{4,5},{5,4},{6,7},{7,6},{8,9},{9,8},{10,11... | collective-permute-start | bytes 16711688 | tf_op jit(solution)/shard_map/ppermute | solution.py:222
  208.4 61.2 %copy-start.21 = (bf16[5120,216]{0,1:T(8,128)(2,1)S(1)}, bf16[5120,216]{0,1:T(8,128)(2,1)}, u32[]{:S(2)}) copy-start(bf16[5120,216]{0,1:T(8,128)(2,1)} %param.31) | copy-start | bytes 6635524
  269.5 4.8 %copy-start.3 = (bf16[1088,2560]{1,0:T(8,128)(2,1)S(1)}, bf16[1088,2560]{1,0:T(8,128)(2,1)}, u32[]{:S(2)}) copy-start(bf16[1088,2560]{1,0:T(8,128)(2,1)} %reshape.433) | copy-start | bytes 16711684
  269.5 4.9 %copy-start.22 = (bf16[5120,216]{0,1:T(8,128)(2,1)S(1)}, bf16[5120,216]{0,1:T(8,128)(2,1)}, u32[]{:S(2)}) copy-start(bf16[5120,216]{0,1:T(8,128)(2,1)} %param.32) | copy-start | bytes 6635524
  269.6 26.7 %collective-permute-start.1 = (bf16[1088,2560]{1,0:T(8,128)(2,1)}, bf16[1088,2560]{1,0:T(8,128)(2,1)}, u32[]{:S(2)}, u32[]{:S(2)}) collective-permute-start(bf16[1088,2560]{1,0:T(8,128)(2,1)} %reshape.435), channel_id=1, source_target_pairs={{0,1},{1,0},{2,3},{3,2},{4,5},{5,4},{6,7},{7,6},{8,9},{9,8},{10,11... | collective-permute-start | bytes 16711688 | tf_op jit(solution)/shard_map/ppermute | solution.py:222
  286.6 63.7 %all-gather.14.cloned.1.call-start = ((), (), s32[]{:S(2)}) async-start(), calls=%async_computation.5 | async-start | bytes 4478976 | tf_op jit(solution)/shard_map/all_gather | solution.py:230
  286.9 4.7 %copy-start.23 = (bf16[5120,216]{0,1:T(8,128)(2,1)S(1)}, bf16[5120,216]{0,1:T(8,128)(2,1)}, u32[]{:S(2)}) copy-start(bf16[5120,216]{0,1:T(8,128)(2,1)} %param.32) | copy-start | bytes 6635524
  325.0 25.3 %copy-start.24 = (bf16[1728,640]{1,0:T(8,128)(2,1)S(1)}, bf16[1728,640]{1,0:T(8,128)(2,1)}, u32[]{:S(2)}) copy-start(bf16[1728,640]{1,0:T(8,128)(2,1)} %param.33) | copy-start | bytes 6635524
  325.0 35.2 %all-to-all-start.1 = ((bf16[16,68,640]{2,1,0:T(8,128)(2,1)}), bf16[16,68,640]{2,1,0:T(8,128)(2,1)}, u32[]{:S(2)}, u32[]{:S(2)}) async-start(bf16[16,68,640]{2,1,0:T(8,128)(2,1)} %all_to_all.24), calls=%async_computation.1 | async-start | bytes 2949120 | tf_op jit(solution)/shard_map/all_to_all | solution.py:232
  356.9 36.1 %copy-start.1 = (bf16[3,4096,128]{2,1,0:T(8,128)(2,1)S(1)}, bf16[3,4096,128]{2,1,0:T(8,128)(2,1)}, u32[]{:S(2)}) copy-start(bf16[3,4096,128]{2,1,0:T(8,128)(2,1)} %param.21) | copy-start | bytes 9437188
  360.3 30.4 %all-to-all-start.2 = ((bf16[16,68,640]{2,1,0:T(8,128)(2,1)}), bf16[16,68,640]{2,1,0:T(8,128)(2,1)}, u32[]{:S(2)}, u32[]{:S(2)}) async-start(bf16[16,68,640]{2,1,0:T(8,128)(2,1)} %all_to_all.26), calls=%async_computation.2 | async-start | bytes 2949120 | tf_op jit(solution)/shard_map/all_to_all | solution.py:232
Sparse Core Ops, SparseCore 0:
  9.5 52.4 all-gather.15
  115.7 21.4 all-gather.9
  140.9 59.5 all-gather.17
  202.5 59.0 all-gather.19
  286.7 30.8 all-gather.11
  319.2 31.0 all-gather.13
where the time goes:
time: 401 us; the launch traced here: 400 us
  waiting for transfers between devices  245 us (61%)
  matrix products  62.1 us (15%)
  local copies, waits for them, and re-layouts  42.2 us (11%)
  starting transfers between devices  19.2 us (5%)
  other arithmetic  16.5 us (4%)
  between operations  14.6 us (4%)
    all_gather x2, waiting for transfers between devices, per_device(): near_rows = lax.all_gather(rows, 'req', axis=0, tiled=True)  112 us
    all_gather x1, waiting for transfers between devices, per_device(): gathered = lax.all_gather(packed, 'req', axis=0, tiled=False)  40.6 us
    all_gather x2, waiting for transfers between devices, per_device(): hidden_block = lax.all_gather(hidden, 'mlp', axis=1, tiled=True)  29 us
    all_to_all x2, waiting for transfers between devices, per_device(): lax.all_to_all(down_partial.astype(jnp.bfloat16), 'req', 0, 0, tiled=True)  21.8 us
    all_gather x1, waiting for transfers between devices, per_device(): lax.all_gather(with_gain, 'mlp', axis=1, tiled=True).astype(jnp.float32)  21.5 us
    all_to_all x1, waiting for transfers between devices, per_device(): lax.all_to_all(head_partial.astype(jnp.bfloat16), 'mlp', 1, 0, tiled=True)  19.3 us
    unnamed x60, local copies, waits for them, and re-layouts  18.1 us
    all_to_all x2, starting transfers between devices, per_device(): lax.all_to_all(down_partial.astype(jnp.bfloat16), 'req', 0, 0, tiled=True)  14.2 us
  transfers between devices with their start and end apart: 11, of which 8 were waited for; matrix products, arithmetic and copies ran while one was open for 20% of the time, Pallas kernels for 0%

commit v1 on v0

--- a/solution.py
+++ b/solution.py
@@ -1,3 +1,4 @@
+import functools
 import math
 import jax
 import jax.numpy as jnp
@@ -9,6 +10,17 @@
 KV = 8
 HD = 128
 NEGATIVE = -1e30
+
+
+def notes_change(xx, row_axis):
+    formed = jax.lax.axis_size(row_axis)
+    m_next = jnp.stack([xx] * formed, 0)
+    z1 = jax.lax.all_to_all(m_next, row_axis, 0, 0)
+    ready = jnp.concatenate(z1, 1)
+    return ready
+
+
+choose_group = functools.partial(notes_change, row_axis="mlp")
 
 
 def absorb(carried, scores, allowed, values, pattern):
@@ -190,7 +202,7 @@
         gain_pieces.append(piece)
         remainder = remainder - piece.astype(jnp.float32)
     with_gain = jnp.concatenate([mixed, jnp.stack(gain_pieces, 0)], 0)
-    gathered_rows = lax.all_gather(with_gain, "mlp", axis=1, tiled=True).astype(jnp.float32)
+    gathered_rows = choose_group(with_gain).astype(jnp.float32)
     mixed_rows = gathered_rows[:rows_here]
     full_gain = (
         gathered_rows[rows_here] + gathered_rows[rows_here + 1] + gathered_rows[rows_here + 2]

time: 401 us -> 402 us (level)
  starting transfers between devices: 19.2 us -> 23.3 us
    all_gather x1 -> x0, waiting for transfers between devices: 21.5 us -> none  [per_device(): lax.all_gather(with_gain, 'mlp', axis=1, tiled=True).astype(jnp.float32)]
    all_to_all x0 -> x1, waiting for transfers between devices: none -> 20.4 us  [notes_change(): z1 = jax.lax.all_to_all(m_next, row_axis, 0, 0)]
    all_to_all x0 -> x1, starting transfers between devices: none -> 4.28 us  [notes_change(): z1 = jax.lax.all_to_all(m_next, row_axis, 0, 0)]
    unnamed x60 -> x59, local copies, waits for them, and re-layouts: 18.1 us -> 18.3 us
where the time goes in v1:
time: 402 us; the launch traced here: 401 us
  waiting for transfers between devices  242 us (60%)
  matrix products  62.1 us (15%)
  local copies, waits for them, and re-layouts  43.7 us (11%)
  starting transfers between devices  23.3 us (6%)
  other arithmetic  15.6 us (4%)
  between operations  14.3 us (4%)
    all_gather x2, waiting for transfers between devices, per_device(): near_rows = lax.all_gather(rows, 'req', axis=0, tiled=True)  110 us
    all_gather x1, waiting for transfers between devices, per_device(): gathered = lax.all_gather(packed, 'req', axis=0, tiled=False)  40.6 us
    all_gather x2, waiting for transfers between devices, per_device(): hidden_block = lax.all_gather(hidden, 'mlp', axis=1, tiled=True)  29 us
    all_to_all x2, waiting for transfers between devices, per_device(): lax.all_to_all(down_partial.astype(jnp.bfloat16), 'req', 0, 0, tiled=True)  21.8 us
    all_to_all x1, waiting for transfers between devices, notes_change(): z1 = jax.lax.all_to_all(m_next, row_axis, 0, 0)  20.4 us
    all_to_all x1, waiting for transfers between devices, per_device(): lax.all_to_all(head_partial.astype(jnp.bfloat16), 'mlp', 1, 0, tiled=True)  19.6 us
    unnamed x59, local copies, waits for them, and re-layouts  18.3 us
    all_to_all x2, starting transfers between devices, per_device(): lax.all_to_all(down_partial.astype(jnp.bfloat16), 'req', 0, 0, tiled=True)  14.2 us
  transfers between devices with their start and end apart: 11, of which 8 were waited for; matrix products, arithmetic and copies ran while one was open for 20% of the time, Pallas kernels for 0%

profile of v1, /device:TPU:0, one launch (start us, length us, event | category | flops | bytes accessed | tf_op | source)
XLA Modules:
  0.0 400.6 jit_solution(16310610305223102010)
XLA Ops:
  6.5 1.8 pad_maximum_fusion
  12.9 1.3 gather_fusion
  15.5 1.3 slice_convert_fusion
  18.9 2.3 fusion.112
  21.4 40.6 %all-gather.13.cloned.1.call-done = bf16[14592,128]{1,0:T(8,128)(2,1)} async-done(((bf16[912,128]{1,0:T(8,128)(2,1)}), bf16[14592,128]{1,0:T(8,128)(2,1)}) %all-gather.13.cloned.1.call-update) | async-done | bytes 3735568 | tf_op jit(solution)/shard_map/all_gather | solution.py:119
  62.0 1.9 fusion.109
  63.9 2.6 fusion.108
  66.5 1.2 copy.26
  68.4 1.2 copy.27
  70.4 1.7 gather_fusion.1
  72.0 2.1 gather_fusion.2
  74.2 1.6 fusion.113
  76.6 2.5 fusion.45
  79.3 1.0 reshape.452
  80.3 1.3 fusion.111
  82.3 1.4 fusion
  85.8 1.4 fusion.52
  88.1 1.3 convolution_convert_fusion
  89.4 1.2 copy.77
  90.6 4.4 %all-to-all-start = ((bf16[136,8,640]{2,0,1:T(8,128)(2,1)}), bf16[136,8,640]{2,0,1:T(8,128)(2,1)S(1)}, u32[]{:S(2)}, u32[]{:S(2)}) async-start(bf16[136,8,640]{2,0,1:T(8,128)(2,1)} %bitcast.178), calls=%async_computation | async-start | bytes 2785280 | tf_op jit(solution)/shard_map/all_to_all | solution.py:194
  95.0 19.6 %all-to-all-done = bf16[136,8,640]{2,0,1:T(8,128)(2,1)S(1)} async-done(((bf16[136,8,640]{2,0,1:T(8,128)(2,1)}), bf16[136,8,640]{2,0,1:T(8,128)(2,1)S(1)}, u32[]{:S(2)}, u32[]{:S(2)}) %all-to-all-start) | async-done | bytes 1392672 | tf_op jit(solution)/shard_map/all_to_all | solution.py:194
  114.9 1.2 stack.11
  116.1 4.3 %all-to-all-start.1 = ((bf16[8,139,640]{2,1,0:T(8,128)(2,1)}), bf16[8,139,640]{2,1,0:T(8,128)(2,1)}, u32[]{:S(2)}, u32[]{:S(2)}) async-start(bf16[8,139,640]{2,1,0:T(8,128)(2,1)} %stack.11), calls=%async_computation.1 | async-start | bytes 2949120 | tf_op jit(solution)/shard_map/all_to_all | solution.py:18
  120.5 20.4 %all-to-all-done.1 = bf16[8,139,640]{2,1,0:T(8,128)(2,1)} async-done(((bf16[8,139,640]{2,1,0:T(8,128)(2,1)}), bf16[8,139,640]{2,1,0:T(8,128)(2,1)}, u32[]{:S(2)}, u32[]{:S(2)}) %all-to-all-start.1) | async-done | bytes 1423392 | tf_op jit(solution)/shard_map/all_to_all | solution.py:18
  140.9 1.6 convert_bitcast_fusion
  145.3 56.1 %all-gather.15.cloned.1.call-done = bf16[16,68,2560]{2,1,0:T(8,128)(2,1)} async-done(((bf16[1,68,2560]{2,1,0:T(8,128)(2,1)}), bf16[16,68,2560]{2,1,0:T(8,128)(2,1)}) %all-gather.15.cloned.1.call-update) | async-done | bytes 5570576 | tf_op jit(solution)/shard_map/all_gather | solution.py:233
  201.4 7.9 %reshape.444 = bf16[1088,2560]{1,0:T(8,128)(2,1)} reshape(bf16[16,68,2560]{2,1,0:T(8,128)(2,1)} %all-gather.15.cloned.1.call-done) | data formatting | bytes 11141120
  209.2 53.5 %all-gather.17.cloned.1.call-done = bf16[16,68,2560]{2,1,0:T(8,128)(2,1)} async-done(((bf16[1,68,2560]{2,1,0:T(8,128)(2,1)}), bf16[16,68,2560]{2,1,0:T(8,128)(2,1)}) %all-gather.17.cloned.1.call-update) | async-done | bytes 5570576 | tf_op jit(solution)/shard_map/all_gather | solution.py:233
  262.7 7.9 %reshape.446 = bf16[1088,2560]{1,0:T(8,128)(2,1)} reshape(bf16[16,68,2560]{2,1,0:T(8,128)(2,1)} %all-gather.17.cloned.1.call-done) | data formatting | bytes 11141120
  270.6 4.7 %fusion.65 = f32[1088,216]{0,1:T(8,128)S(1)} fusion(bf16[1088,2560]{1,0:T(8,128)(2,1)} %reshape.444, bf16[5120,216]{0,1:T(8,128)(2,1)S(1)} %copy-done.20, s32[]{:T(128)S(6)} %select_n.78), kind=kOutput, calls=%fused_computation.74 | convolution fusion | flops 1203240960 | bytes 7616516 | tf_op jit(solution)/shard_map/dot_general | solution.py:235
  275.5 2.0 fusion.59
  277.5 4.6 %convolution_add_fusion.3 = f32[1088,216]{0,1:T(8,128)S(1)} fusion(f32[1088,216]{0,1:T(8,128)S(1)} %fusion.65, bf16[1088,2560]{1,0:T(8,128)(2,1)} %collective-permute-done, bf16[5120,216]{0,1:T(8,128)(2,1)S(1)} %copy-done.20, s32[]{:T(128)S(6)} %select_n.79), kind=kOutput, calls=%fused_computation.33 | convolution fusion | flops 1203475968 | bytes 8611844 | tf_op jit(solution)/shard_map/dot_general | solution.py:235
  282.1 5.5 %fusion.13 = bf16[1088,216]{0,1:T(8,128)(2,1)} fusion(f32[1088,216]{0,1:T(8,128)S(1)} %fusion.59, bf16[1088,2560]{1,0:T(8,128)(2,1)} %collective-permute-done, f32[1088,216]{0,1:T(8,128)S(1)} %convolution_add_fusion.3, bf16[5120,216]{0,1:T(8,128)(2,1)S(1)} %copy-done.21, s32[]{:T(128)S(6)} %select_n.79), kind=kOutput, calls=%fused_computation.34 | convolution fusion | flops 1204886016 | bytes 9137156 | tf_op jit(solution)/shard_map/dot_general | solution.py:238
  287.9 4.7 %fusion.63 = f32[1088,216]{0,1:T(8,128)S(1)} fusion(bf16[1088,2560]{1,0:T(8,128)(2,1)} %reshape.446, bf16[5120,216]{0,1:T(8,128)(2,1)S(1)} %copy-done.20, s32[]{:T(128)S(6)} %select_n.78), kind=kOutput, calls=%fused_computation.72 | convolution fusion | flops 1203240960 | bytes 7616516 | tf_op jit(solution)/shard_map/dot_general | solution.py:235
  292.7 4.6 %fusion.57 = f32[1088,216]{0,1:T(8,128)S(1)} fusion(bf16[1088,2560]{1,0:T(8,128)(2,1)} %reshape.446, bf16[5120,216]{0,1:T(8,128)(2,1)S(1)} %copy-done.22, s32[]{:T(128)S(6)} %select_n.78), kind=kOutput, calls=%fused_computation.66 | convolution fusion | flops 1203240960 | bytes 7616516 | tf_op jit(solution)/shard_map/dot_general | solution.py:238
  297.3 5.0 %convolution_add_fusion.1 = f32[1088,216]{0,1:T(8,128)S(1)} fusion(f32[1088,216]{0,1:T(8,128)S(1)} %fusion.63, bf16[1088,2560]{1,0:T(8,128)(2,1)} %collective-permute-done.1, bf16[5120,216]{0,1:T(8,128)(2,1)S(1)} %copy-done.20, s32[]{:T(128)S(6)} %select_n.79), kind=kOutput, calls=%fused_computation.30 | convolution fusion | flops 1203475968 | bytes 8611844 | tf_op jit(solution)/shard_map/dot_general | solution.py:235
  302.2 5.5 %fusion.14 = bf16[1088,216]{0,1:T(8,128)(2,1)} fusion(f32[1088,216]{0,1:T(8,128)S(1)} %fusion.57, bf16[1088,2560]{1,0:T(8,128)(2,1)} %collective-permute-done.1, f32[1088,216]{0,1:T(8,128)S(1)} %convolution_add_fusion.1, bf16[5120,216]{0,1:T(8,128)(2,1)S(1)} %copy-done.22, s32[]{:T(128)S(6)} %select_n.79), kind=kOutput, calls=%fused_computation.35 | convolution fusion | flops 1204886016 | bytes 9137156 | tf_op jit(solution)/shard_map/dot_general | solution.py:238
  307.8 10.9 %all-gather.9.cloned.1.call-done = bf16[1088,1728]{0,1:T(8,128)(2,1)} async-done(((bf16[1088,216]{0,1:T(8,128)(2,1)}), bf16[1088,1728]{0,1:T(8,128)(2,1)}) %all-gather.9.cloned.1.call-update) | async-done | bytes 3760144 | tf_op jit(solution)/shard_map/all_gather | solution.py:242
  318.7 6.1 %convolution_convert_fusion.2 = bf16[1088,640]{1,0:T(8,128)(2,1)S(1)} fusion(bf16[1088,1728]{0,1:T(8,128)(2,1)} %all-gather.9.cloned.1.call-done, bf16[1728,640]{1,0:T(8,128)(2,1)} %param.33), kind=kOutput, calls=%fused_computation.11 | convolution fusion | flops 2407178240 | bytes 7364608 | tf_op jit(solution)/shard_map/dot_general | solution.py:243
  324.8 1.3 all_to_all.28
  326.1 7.2 %all-to-all-start.2 = ((bf16[16,68,640]{2,1,0:T(8,128)(2,1)}), bf16[16,68,640]{2,1,0:T(8,128)(2,1)}, u32[]{:S(2)}, u32[]{:S(2)}) async-start(bf16[16,68,640]{2,1,0:T(8,128)(2,1)} %all_to_all.28), calls=%async_computation.2 | async-start | bytes 2949120 | tf_op jit(solution)/shard_map/all_to_all | solution.py:244
  333.3 18.1 %all-gather.11.cloned.1.call-done = bf16[1088,1728]{0,1:T(8,128)(2,1)} async-done(((bf16[1088,216]{0,1:T(8,128)(2,1)}), bf16[1088,1728]{0,1:T(8,128)(2,1)}) %all-gather.11.cloned.1.call-update) | async-done | bytes 3760144 | tf_op jit(solution)/shard_map/all_gather | solution.py:242
  351.4 6.6 %convolution_convert_fusion.1 = bf16[1088,640]{1,0:T(8,128)(2,1)} fusion(bf16[1088,1728]{0,1:T(8,128)(2,1)} %all-gather.11.cloned.1.call-done, bf16[1728,640]{1,0:T(8,128)(2,1)S(1)} %copy-done.23), kind=kOutput, calls=%fused_computation.10 | convolution fusion | flops 2407178240 | bytes 7364608 | tf_op jit(solution)/shard_map/dot_general | solution.py:243
  357.9 3.4 all_to_all.30
  361.3 7.0 %all-to-all-start.3 = ((bf16[16,68,640]{2,1,0:T(8,128)(2,1)}), bf16[16,68,640]{2,1,0:T(8,128)(2,1)}, u32[]{:S(2)}, u32[]{:S(2)}) async-start(bf16[16,68,640]{2,1,0:T(8,128)(2,1)} %all_to_all.30), calls=%async_computation.3 | async-start | bytes 2949120 | tf_op jit(solution)/shard_map/all_to_all | solution.py:244
  368.4 1.6 convert_reduce_fusion.1
  370.0 21.8 %all-to-all-done.3 = bf16[16,68,640]{2,1,0:T(8,128)(2,1)} async-done(((bf16[16,68,640]{2,1,0:T(8,128)(2,1)}), bf16[16,68,640]{2,1,0:T(8,128)(2,1)}, u32[]{:S(2)}, u32[]{:S(2)}) %all-to-all-start.3) | async-done | bytes 1392672 | tf_op jit(solution)/shard_map/all_to_all | solution.py:244
  391.7 1.6 convert_reduce_fusion
  (114 shorter events, 17.7 us)
Async XLA Ops:
  6.5 12.3 %copy-start = (bf16[3,4096,128]{2,1,0:T(8,128)(2,1)S(1)}, bf16[3,4096,128]{2,1,0:T(8,128)(2,1)}, u32[]{:S(2)}) copy-start(bf16[3,4096,128]{2,1,0:T(8,128)(2,1)} %param.21) | copy-start | bytes 9437188
  6.5 55.5 %all-gather.13.cloned.1.call-start = ((), (), s32[]{:S(2)}) async-start(), calls=%async_computation.6 | async-start | bytes 3969024 | tf_op jit(solution)/shard_map/all_gather | solution.py:119
  10.1 8.0 %copy-start.13 = (bf16[3,5,128]{2,1,0:T(8,128)(2,1)}, bf16[3,5,128]{2,1,0:T(8,128)(2,1)S(1)}, u32[]{:S(2)}) copy-start(bf16[3,5,128]{2,1,0:T(8,128)(2,1)S(1)} %reshape.393) | copy-start | bytes 11524
  68.4 1.9 copy-start.3
  68.4 5.7 %copy-start.12 = (pred[3,1024]{1,0:T(4,128)(4,1)S(1)}, pred[3,1024]{1,0:T(4,128)(4,1)}, u32[]{:S(2)}) copy-start(pred[3,1024]{1,0:T(4,128)(4,1)} %iota_compare_fusion.2) | copy-start | bytes 9220
  68.4 5.8 %copy-start.14 = (bf16[3,5,128]{2,1,0:T(8,128)(2,1)S(1)}, bf16[3,5,128]{2,1,0:T(8,128)(2,1)}, u32[]{:S(2)}) copy-start(bf16[3,5,128]{2,1,0:T(8,128)(2,1)} %copy-done.13) | copy-start | bytes 11524
  69.6 6.2 %copy-start.15 = (f32[3,5]{1,0:T(4,128)S(1)}, f32[3,5]{1,0:T(4,128)}, u32[]{:S(2)}) copy-start(f32[3,5]{1,0:T(4,128)} %get-tuple-element.31) | copy-start | bytes 184
  69.6 6.2 %copy-start.18 = (f32[3,1,5]{2,1,0:T(1,128)S(1)}, f32[3,1,5]{2,1,0:T(1,128)}, u32[]{:S(2)}) copy-start(f32[3,1,5]{2,1,0:T(1,128)} %fusion.89) | copy-start | bytes 184
  70.4 6.2 %copy-start.17 = (f32[3,128]{1,0:T(4,128)S(1)}, f32[3,128]{1,0:T(4,128)}, u32[]{:S(2)}) copy-start(f32[3,128]{1,0:T(4,128)} %slice_convert_fusion) | copy-start | bytes 4612
  74.2 4.9 %copy-start.5 = (bf16[16,133,128]{2,1,0:T(8,128)(2,1)S(1)}, bf16[16,133,128]{2,1,0:T(8,128)(2,1)}, u32[]{:S(2)}) copy-start(bf16[16,133,128]{2,1,0:T(8,128)(2,1)} %get-tuple-element.8) | copy-start | bytes 1634308
  76.3 3.0 copy-start.4
  76.6 3.7 copy-start.6
  80.3 1.3 copy-start.7
  80.3 1.4 copy-start.8
  80.3 1.4 copy-start.16
  83.8 1.0 copy-start.10
  84.8 1.0 copy-start.9
  84.8 2.6 slice-start
  85.8 2.3 slice-start.1
  89.3 5.6 %copy-start.19 = (f32[640]{0:T(1024)S(1)}, f32[640]{0:T(1024)}, u32[]{:S(2)}) copy-start(f32[640]{0:T(1024)} %param.30) | copy-start | bytes 7684
  90.6 24.2 %copy-start.11 = (bf16[136,640]{1,0:T(8,128)(2,1)S(1)}, bf16[136,640]{1,0:T(8,128)(2,1)}, u32[]{:S(2)}) copy-start(bf16[136,640]{1,0:T(8,128)(2,1)} %param.17) | copy-start | bytes 522244
  90.6 24.0 %all-to-all-start = ((bf16[136,8,640]{2,0,1:T(8,128)(2,1)}), bf16[136,8,640]{2,0,1:T(8,128)(2,1)S(1)}, u32[]{:S(2)}, u32[]{:S(2)}) async-start(bf16[136,8,640]{2,0,1:T(8,128)(2,1)} %bitcast.178), calls=%async_computation | async-start | bytes 2785280 | tf_op jit(solution)/shard_map/all_to_all | solution.py:194
  116.1 24.8 %all-to-all-start.1 = ((bf16[8,139,640]{2,1,0:T(8,128)(2,1)}), bf16[8,139,640]{2,1,0:T(8,128)(2,1)}, u32[]{:S(2)}, u32[]{:S(2)}) async-start(bf16[8,139,640]{2,1,0:T(8,128)(2,1)} %stack.11), calls=%async_computation.1 | async-start | bytes 2949120 | tf_op jit(solution)/shard_map/all_to_all | solution.py:18
  120.4 81.0 %all-gather.15.cloned.1.call-start = ((), (), s32[]{:S(2)}) async-start(), calls=%async_computation.7 | async-start | bytes 6266880 | tf_op jit(solution)/shard_map/all_gather | solution.py:233
  144.5 118.2 %all-gather.17.cloned.1.call-start = ((), (), s32[]{:S(2)}) async-start(), calls=%async_computation.8 | async-start | bytes 6266880 | tf_op jit(solution)/shard_map/all_gather | solution.py:233
  145.2 173.4 %all-gather.9.cloned.1.call-start = ((), (), s32[]{:S(2)}) async-start(), calls=%async_computation.4 | async-start | bytes 4478976 | tf_op jit(solution)/shard_map/all_gather | solution.py:242
  209.2 68.2 %collective-permute-start = (bf16[1088,2560]{1,0:T(8,128)(2,1)}, bf16[1088,2560]{1,0:T(8,128)(2,1)}, u32[]{:S(2)}, u32[]{:S(2)}) collective-permute-start(bf16[1088,2560]{1,0:T(8,128)(2,1)} %reshape.444), channel_id=1, source_target_pairs={{0,1},{1,0},{2,3},{3,2},{4,5},{5,4},{6,7},{7,6},{8,9},{9,8},{10,11... | collective-permute-start | bytes 16711688 | tf_op jit(solution)/shard_map/ppermute | solution.py:234
  209.2 61.3 %copy-start.20 = (bf16[5120,216]{0,1:T(8,128)(2,1)S(1)}, bf16[5120,216]{0,1:T(8,128)(2,1)}, u32[]{:S(2)}) copy-start(bf16[5120,216]{0,1:T(8,128)(2,1)} %param.31) | copy-start | bytes 6635524
  270.6 4.7 %copy-start.2 = (bf16[1088,2560]{1,0:T(8,128)(2,1)S(1)}, bf16[1088,2560]{1,0:T(8,128)(2,1)}, u32[]{:S(2)}) copy-start(bf16[1088,2560]{1,0:T(8,128)(2,1)} %reshape.444) | copy-start | bytes 16711684
  270.6 4.9 %copy-start.21 = (bf16[5120,216]{0,1:T(8,128)(2,1)S(1)}, bf16[5120,216]{0,1:T(8,128)(2,1)}, u32[]{:S(2)}) copy-start(bf16[5120,216]{0,1:T(8,128)(2,1)} %param.32) | copy-start | bytes 6635524
  270.6 26.7 %collective-permute-start.1 = (bf16[1088,2560]{1,0:T(8,128)(2,1)}, bf16[1088,2560]{1,0:T(8,128)(2,1)}, u32[]{:S(2)}, u32[]{:S(2)}) collective-permute-start(bf16[1088,2560]{1,0:T(8,128)(2,1)} %reshape.446), channel_id=1, source_target_pairs={{0,1},{1,0},{2,3},{3,2},{4,5},{5,4},{6,7},{7,6},{8,9},{9,8},{10,11... | collective-permute-start | bytes 16711688 | tf_op jit(solution)/shard_map/ppermute | solution.py:234
  287.6 63.7 %all-gather.11.cloned.1.call-start = ((), (), s32[]{:S(2)}) async-start(), calls=%async_computation.5 | async-start | bytes 4478976 | tf_op jit(solution)/shard_map/all_gather | solution.py:242
  287.9 4.7 %copy-start.22 = (bf16[5120,216]{0,1:T(8,128)(2,1)S(1)}, bf16[5120,216]{0,1:T(8,128)(2,1)}, u32[]{:S(2)}) copy-start(bf16[5120,216]{0,1:T(8,128)(2,1)} %param.32) | copy-start | bytes 6635524
  326.1 25.3 %copy-start.23 = (bf16[1728,640]{1,0:T(8,128)(2,1)S(1)}, bf16[1728,640]{1,0:T(8,128)(2,1)}, u32[]{:S(2)}) copy-start(bf16[1728,640]{1,0:T(8,128)(2,1)} %param.33) | copy-start | bytes 6635524
  326.1 35.2 %all-to-all-start.2 = ((bf16[16,68,640]{2,1,0:T(8,128)(2,1)}), bf16[16,68,640]{2,1,0:T(8,128)(2,1)}, u32[]{:S(2)}, u32[]{:S(2)}) async-start(bf16[16,68,640]{2,1,0:T(8,128)(2,1)} %all_to_all.28), calls=%async_computation.2 | async-start | bytes 2949120 | tf_op jit(solution)/shard_map/all_to_all | solution.py:244
  357.9 36.1 %copy-start.1 = (bf16[3,4096,128]{2,1,0:T(8,128)(2,1)S(1)}, bf16[3,4096,128]{2,1,0:T(8,128)(2,1)}, u32[]{:S(2)}) copy-start(bf16[3,4096,128]{2,1,0:T(8,128)(2,1)} %param.21) | copy-start | bytes 9437188
  361.3 30.4 %all-to-all-start.3 = ((bf16[16,68,640]{2,1,0:T(8,128)(2,1)}), bf16[16,68,640]{2,1,0:T(8,128)(2,1)}, u32[]{:S(2)}, u32[]{:S(2)}) async-start(bf16[16,68,640]{2,1,0:T(8,128)(2,1)} %all_to_all.30), calls=%async_computation.3 | async-start | bytes 2949120 | tf_op jit(solution)/shard_map/all_to_all | solution.py:244
Sparse Core Ops, SparseCore 0:
  9.5 52.4 all-gather.12
  144.6 56.7 all-gather.14
  203.6 59.0 all-gather.16
  287.8 30.8 all-gather.8
  320.3 31.0 all-gather.10
